TPU v7x, 32 devices: a whole 2x2x4 slice. The times are simulated.
32 devices in a mesh: row: 4 (over z), col: 8 (over y, x, core).
Axes of the slice: x: 2, y: 2, z: 4, core: 2. Of those that a mesh axis runs over, the one named last changes fastest.
Arguments:
- xn: bfloat16 [256, 2048], P('col', 'row'), may hold values from -6 to 6
- w_qkv: bfloat16 [2048, 6144], P('row', 'col'), may hold values from -0.125 to 0.125
- w_out: bfloat16 [2048, 2048], P('col', 'row'), may hold values from -0.125 to 0.125
- pool: bfloat16 [1024, 64, 4096], P('row', None, 'col'), may hold values from -136 to 136
- page_table: int32 [256, 64], P('row'), may hold values from 0 to 271
- lengths: int32 [256], P('row'), may hold values from 1 to 4096, 24576 in all
- mig_src: int32 [64], replicated, may hold values from 0 to 1023, as said below
- deal: int32 [256], replicated, may hold values from 0 to 255, each once
Outputs:
- attended: bfloat16 [256, 2048], P('col', 'row')
- landed: bfloat16 [64, 64, 4096], P('row', None, 'col')
Inputs may be any that keep to these rules, and one draw needn't show every extreme that they name: `page_table`: page ids of a request refer to its own row block: below 256 its pool pages, from 256 its landing slots. `lengths`: the longest request has exactly 4096 cache tokens. `mig_src`: slot d belongs to row block d // 16; its source page lies in the pool pages of another row block. `deal`: a permutation of the requests.
All inputs are finite; a program needn't handle non-finite values. No bound on the sum of `lengths` on one device may be relied on, other than what follows from the above.
Results may differ from a plain program's by a relative error of at most 0.02.
Values may be sent and summed in bfloat16 or wider, within the bound.
No kernel may reach another device: no remote copies, remote signals or barrier semaphores. Data moves between devices by JAX's collectives and lax.ppermute only.
A program may use at most 128 MiB of HBM per device.

v0:
```python
import jax
import jax.numpy as jnp
from jax import lax
from jax.sharding import PartitionSpec as P

HEAD_DIM = 64
PAGE = 64


theta_base = 130000.0
neg_large = -1e30


def rotate(values, positions):
    half = values.shape[-1] // 2
    freqs = theta_base ** (-(jnp.arange(half, dtype=jnp.float32) * 2.0 / values.shape[-1]))
    angles = positions.astype(jnp.float32)[:, None, None] * freqs[None, None, :]
    cosine = jnp.cos(angles)
    sine = jnp.sin(angles)
    first = values[..., :half]
    second = values[..., half:]
    return jnp.concatenate(
        [first * cosine - second * sine, second * cosine + first * sine], axis=-1
    )


def attend(query, key_new, value_new, table, lens, key_pool, value_pool):
    req_count = query.shape[0]
    heads_here = query.shape[1]
    pages_all = table.shape[1]
    pages_block = min(pages_all, max(1, 512 // PAGE))
    block_len = pages_block * PAGE
    longest = jnp.max(lens)
    block_count = (longest + block_len - 1) // block_len
    positions = jnp.arange(block_len, dtype=jnp.int32)

    def score_block(block_no, scores):
        page_ids = lax.dynamic_slice_in_dim(table, block_no * pages_block, pages_block, 1)
        keys = key_pool[page_ids].reshape(req_count, block_len, heads_here, HEAD_DIM)
        block_scores = (
            jnp.einsum("rhe,rthe->rht", query, keys, preferred_element_type=jnp.float32) * 0.125
        )
        valid = (block_no * block_len + positions)[None, None, :] < lens[:, None, None]
        block_scores = jnp.where(valid, block_scores, neg_large)
        return lax.dynamic_update_slice_in_dim(scores, block_scores, block_no * block_len, 2)

    initial = jnp.full((req_count, heads_here, pages_all * PAGE), neg_large, jnp.float32)
    scores = lax.fori_loop(0, block_count, score_block, initial)
    score_new = jnp.sum(query.astype(jnp.float32) * key_new.astype(jnp.float32), axis=-1) * 0.125
    top = jnp.maximum(jnp.max(scores, axis=2), score_new)
    expo_new = jnp.exp(score_new - top)
    total = jnp.sum(jnp.exp(scores - top[..., None]), axis=2) + expo_new

    def value_block(block_no, numer):
        block_scores = lax.dynamic_slice_in_dim(scores, block_no * block_len, block_len, 2)
        weights = jnp.exp(block_scores - top[..., None]).astype(jnp.bfloat16)
        page_ids = lax.dynamic_slice_in_dim(table, block_no * pages_block, pages_block, 1)
        values = value_pool[page_ids].reshape(req_count, block_len, heads_here, HEAD_DIM)
        return numer + jnp.einsum(
            "rht,rthe->rhe", weights, values, preferred_element_type=jnp.float32
        )

    numer = lax.fori_loop(
        0, block_count, value_block, jnp.zeros((req_count, heads_here, HEAD_DIM), jnp.float32)
    )
    weight_new = lax.optimization_barrier(expo_new.astype(jnp.bfloat16)).astype(jnp.float32)
    numer = numer + weight_new[..., None] * value_new.astype(jnp.float32)
    return (numer / total[..., None]).astype(jnp.bfloat16)


def on_device(xn, w_qkv, w_out, pool, page_table, lengths, mig_src, deal):
    heads_here = w_out.shape[0] // HEAD_DIM
    rows_all = xn.shape[0] * lax.axis_size("col")
    row_count = lax.axis_size("row")
    req_row = rows_all // row_count
    inverse = jnp.zeros((rows_all,), jnp.int32).at[deal].set(jnp.arange(rows_all, dtype=jnp.int32))
    gathered = lax.all_gather(xn, "col", axis=0, tiled=True)
    chosen = inverse
    projected = lax.psum_scatter(
        jnp.dot(jnp.take(gathered, chosen, axis=0), w_qkv, preferred_element_type=jnp.float32),
        "row",
        scatter_dimension=0,
        tiled=True,
    )
    projected = projected.reshape(req_row, heads_here, 3, HEAD_DIM)
    query = rotate(projected[:, :, 0], lengths).astype(jnp.bfloat16)
    key_new = rotate(projected[:, :, 1], lengths).astype(jnp.bfloat16)
    value_new = projected[:, :, 2].astype(jnp.bfloat16)
    my_row = lax.axis_index("row")
    pool_dev = pool.shape[0]
    land_dev = mig_src.shape[0] // row_count
    source_row = mig_src // pool_dev
    local_page = jnp.clip(mig_src - my_row * pool_dev, 0, pool_dev - 1)
    outgoing = jnp.where(
        (source_row == my_row)[:, None, None],
        jnp.take(pool, local_page, axis=0),
        jnp.zeros((), jnp.bfloat16),
    )
    outgoing = outgoing.reshape(row_count, land_dev, pool.shape[1], pool.shape[2])
    received = lax.all_to_all(outgoing, "row", split_axis=0, concat_axis=0, tiled=True)
    my_sources = lax.dynamic_slice_in_dim(source_row, my_row * land_dev, land_dev)
    landed = received[my_sources, jnp.arange(land_dev)]
    combined = jnp.concatenate([pool, landed], axis=0)
    combined = combined.reshape(combined.shape[0], PAGE, heads_here, 2, HEAD_DIM)
    key_pool = combined[:, :, :, 0]
    value_pool = combined[:, :, :, 1]
    mixed = attend(query, key_new, value_new, page_table, lengths, key_pool, value_pool)
    mixed = mixed.reshape(req_row, heads_here * HEAD_DIM)
    mixed_all = lax.all_gather(mixed, "row", axis=0, tiled=True)
    chosen = deal
    attended = lax.psum_scatter(
        jnp.dot(
            jnp.take(mixed_all, chosen, axis=0), w_out, preferred_element_type=jnp.float32
        ).astype(jnp.bfloat16),
        "col",
        scatter_dimension=0,
        tiled=True,
    )
    return (attended, landed)


def solution(mesh):
    placed = (
        P("col", "row"),
        P("row", "col"),
        P("col", "row"),
        P("row", None, "col"),
        P("row", None),
        P("row"),
        P(),
        P(),
    )
    return jax.shard_map(
        on_device,
        mesh=mesh,
        in_specs=placed,
        out_specs=(P("col", "row"), P("row", None, "col")),
        check_vma=False,
    )
```

profile of v0, /device:TPU:0, one launch (start us, length us, event | category | flops | bytes accessed | tf_op | source)
XLA Modules:
  0.0 1240.1 jit_solution(6100421944838568326)
XLA Ops:
  7.2 0.7 broadcast_compare_fusion.1
  8.1 8.5 gather_fusion.2
  16.7 3.9 select_select_fusion
  20.6 6.3 all-to-all-start
  26.9 1.4 scatter_custom_fusion
  28.3 9.4 all_gather.6
  37.7 1.2 gather_fusion.4
  38.9 1.3 fusion.11
  40.3 0.6 fusion.32
  41.6 25.0 %copy.13 = bf16[256,64,512]{0,2,1:T(8,128)(2,1)} copy(bf16[256,64,512]{2,1,0:T(8,128)(2,1)} %param.15) | data formatting | bytes 33554432 | tf_op args[3]
  66.7 0.6 pad_clamp_fusion.2
  67.3 0.5 compare_and_fusion.2
  67.8 0.2 multiply_cosine_fusion
  68.0 23.6 %reduce-scatter.3.cloned.1.call-done = f32[64,768]{1,0:T(8,128)} async-done(((f32[256,768]{1,0:T(8,128)}), f32[64,768]{1,0:T(8,128)}) %reduce-scatter.3.cloned.1.call-update) | async-done | bytes 196624 | tf_op jit(solution)/shard_map/reduce_scatter | solution.py:79
  91.6 1.2 reshape.154
  92.8 0.2 fusion.31
  93.0 0.2 subtract_convert_fusion.1
  93.2 0.9 multiply_reduce_fusion
  94.1 0.8 fusion.14
  94.9 38.0 %all-to-all-done = bf16[4,16,64,512]{3,2,1,0:T(8,128)(2,1)} async-done(((bf16[4,16,64,512]{3,2,1,0:T(8,128)(2,1)}), bf16[4,16,64,512]{3,2,1,0:T(8,128)(2,1)}, u32[]{:S(2)}, u32[]{:S(2)}) %all-to-all-start) | async-done | bytes 4194336 | tf_op jit(solution)/shard_map/all_to_all | solution.py:100
  132.9 2.8 gather_fusion.3
  135.7 5.9 copy.14
  141.7 17.0 %pad_maximum_fusion = bf16[272,64,512]{0,2,1:T(8,128)(2,1)} fusion(bf16[16,64,512]{0,2,1:T(8,128)(2,1)} %copy.14, bf16[256,64,512]{0,2,1:T(8,128)(2,1)} %copy.13), kind=kLoop, calls=%fused_computation.25 | loop fusion | flops 35651584 | bytes 35651584 | tf_op jit(solution)/shard_map/concatenate | solution.py:103
  158.7 21.7 %slice_bitcast_fusion = (bf16[272,64,4,64]{0,3,2,1:T(8,128)(2,1)}, bf16[272,64,4,64]{0,3,2,1:T(8,128)(2,1)}) fusion(bf16[272,64,4,2,64]{0,4,3,2,1:T(8,128)(2,1)} %bitcast.48), kind=kLoop, calls=%fused_computation.26 | loop fusion | bytes 35651584 | tf_op jit(solution)/shard_map/squeeze | solution.py:106
  180.4 26.5 %copy.16 = bf16[272,64,4,64]{3,2,1,0:T(4,128)(2,1)} copy(bf16[272,64,4,64]{0,3,2,1:T(8,128)(2,1)} %get-tuple-element.151) | data formatting | bytes 17825792
  206.9 3.0 broadcast_in_dim.94
  209.9 58.7 %while.22 = (s32[]{:T(128)}, f32[64,4,4096]{2,1,0:T(4,128)}, s32[]{:T(128)}, s32[64]{0:T(128)S(1)}, s32[64,64]{1,0:T(8,128)S(1)}, /*index=5*/bf16[272,64,4,64]{3...) while((s32[]{:T(128)}, f32[64,4,4096]{2,1,0:T(4,128)}, ...), condition=%wide.region_4.5_spmd.clone, body=%wide.region_3.4_spmd.clone.sunk | while | flops 17075208 | bytes 52023780 | solution.py:48
  210.0 0.1 reshape.247
  210.1 42.6 %gather_fusion.1 = bf16[512,64,4,64]{3,2,1,0:T(4,128)(2,1)} fusion(bf16[272,64,4,64]{3,2,1,0:T(4,128)(2,1)} %get-tuple-element.287, s32[1024]{0:T(1024)S(1)} %pad_clamp_fusion.8), kind=kCustom, calls=%fused_computation.clone.clone.1 | custom fusion | bytes 33556480 | tf_op jit(solution)/shard_map/while/body/gather | solution.py:39
  252.7 14.6 %fusion.49 = f32[64,4,1,512]{3,2,1,0:T(1,128)S(1)} fusion(bf16[64,512,4,64]{3,2,1,0:T(4,128)(2,1)} %bitcast.47, bf16[64,4,64,1]{2,1,0,3:T(4,128)(2,1)S(1)} %bitcast.54), kind=kOutput, calls=%fused_computation.15.clone.1 | convolution fusion | flops 16777216 | bytes 17334272 | tf_op jit(solution)/shard_map/while/body/rhe,rthe->rht/dot_general | solution.py:41
  267.3 0.1 broadcast_compare_fusion.3
  267.4 1.1 fusion.50
  268.6 2.8 reduce_max.19
  271.4 3.7 exponential_reduce_fusion
  275.1 0.6 fusion.21
  275.7 0.6 convert_element_type.39
  276.3 26.5 %copy.17 = bf16[272,64,4,64]{3,2,1,0:T(4,128)(2,1)} copy(bf16[272,64,4,64]{0,3,2,1:T(8,128)(2,1)} %get-tuple-element.150) | data formatting | bytes 17825792 | tf_op jit(solution)/shard_map/while | solution.py:63
  302.9 59.4 %while.21 = (s32[]{:T(128)}, f32[64,4,64]{2,1,0:T(4,128)S(1)}, s32[]{:T(128)}, f32[64,4,4096]{2,1,0:T(4,128)}, f32[64,4]{1,0:T(8,128)S(1)}, /*index=5*/s32[64,64...) while((s32[]{:T(128)}, f32[64,4,64]{2,1,0:T(4,128)S(1)}, ...), condition=%wide.region_8.9_spmd, body=%wide.region_7.8_spmd.sunk | while | flops 17058312 | bytes 51660000 | solution.py:63
  303.2 0.1 reshape.244
  303.3 42.6 %gather_fusion = bf16[512,64,4,64]{3,2,1,0:T(4,128)(2,1)} fusion(bf16[272,64,4,64]{3,2,1,0:T(4,128)(2,1)} %get-tuple-element.327, s32[1024]{0:T(1024)S(1)} %pad_clamp_fusion.7), kind=kCustom, calls=%fused_computation.1.clone.1 | custom fusion | bytes 33556480 | tf_op jit(solution)/shard_map/while/body/gather | solution.py:58
  345.9 1.2 fusion.45
  347.2 15.0 %fusion.46 = f32[64,4,1,64]{3,2,1,0:T(1,128)S(1)} fusion(bf16[64,512,4,64]{3,2,1,0:T(4,128)(2,1)} %bitcast.46, bf16[64,4,512,1]{2,1,0,3:T(4,128)(2,1)S(1)} %fusion.45), kind=kOutput, calls=%fused_computation.8.clone.1 | convolution fusion | flops 16777216 | bytes 17104896 | tf_op jit(solution)/shard_map/while/body/rht,rthe->rhe/dot_general | solution.py:59
  362.3 0.2 fusion.18
  362.5 0.1 reshape.155
  362.6 832.9 %all_gather.7 = bf16[256,256]{1,0:T(8,128)(2,1)S(1)} all-gather(bf16[64,256]{1,0:T(8,128)(2,1)S(1)} %reshape.155), channel_id=1, replica_groups=mesh['row'=4,'col'=8] {'row'}, dimensions={0}, use_global_device_ids=true | all-gather | bytes 163840 | tf_op jit(solution)/shard_map/all_gather | solution.py:109
  1195.6 1.3 gather_fusion.5
  1196.9 1.0 convolution_convert_fusion
  1197.9 35.4 %reduce-scatter.5.cloned.1.call-done = bf16[32,512]{1,0:T(8,128)(2,1)} async-done(((bf16[256,512]{1,0:T(8,128)(2,1)}), bf16[32,512]{1,0:T(8,128)(2,1)}) %reduce-scatter.5.cloned.1.call-update) | async-done | bytes 32784 | tf_op jit(solution)/shard_map/reduce_scatter | solution.py:111
  (50 shorter events, 0.7 us)
Async XLA Ops:
  7.2 31.7 %copy-start = (bf16[512,768]{1,0:T(8,128)(2,1)S(1)}, bf16[512,768]{1,0:T(8,128)(2,1)}, u32[]{:S(2)}) copy-start(bf16[512,768]{1,0:T(8,128)(2,1)} %param.13) | copy-start | bytes 2359300
  7.2 19.7 %copy-start.12 = (s32[256]{0:T(256)S(1)}, s32[256]{0:T(256)}, u32[]{:S(2)}) copy-start(s32[256]{0:T(256)} %param.19) | copy-start | bytes 3076
  7.2 21.1 %copy-start.9 = (bf16[32,512]{1,0:T(8,128)(2,1)S(1)}, bf16[32,512]{1,0:T(8,128)(2,1)}, u32[]{:S(2)}) copy-start(bf16[32,512]{1,0:T(8,128)(2,1)} %param.12) | copy-start | bytes 98308
  7.2 33.1 %copy-start.10 = (s32[64]{0:T(128)S(1)}, s32[64]{0:T(128)}, u32[]{:S(2)}) copy-start(s32[64]{0:T(128)} %param.17) | copy-start | bytes 772
  20.6 112.4 %all-to-all-start = ((bf16[4,16,64,512]{3,2,1,0:T(8,128)(2,1)}), bf16[4,16,64,512]{3,2,1,0:T(8,128)(2,1)}, u32[]{:S(2)}, u32[]{:S(2)}) async-start(bf16[4,16,64,512]{3,2,1,0:T(8,128)(2,1)} %select_select_fusion), calls=%async_computation | async-start | bytes 8388608 | tf_op jit(solution)/shard_map/all_to_all | solution.py:100
  26.9 64.7 %reduce-scatter.3.cloned.1.call-start = ((), (), s32[]{:S(2)}) async-start(), calls=%async_computation.3 | async-start | bytes 983040 | tf_op jit(solution)/shard_map/reduce_scatter | solution.py:79
  40.2 1193.1 %reduce-scatter.5.cloned.1.call-start = ((), (), s32[]{:S(2)}) async-start(), calls=%async_computation.4 | async-start | bytes 294912 | tf_op jit(solution)/shard_map/reduce_scatter | solution.py:111
  135.7 23.0 %copy-start.2 = (bf16[16,64,512]{2,1,0:T(8,128)(2,1)}, bf16[16,64,512]{2,1,0:T(8,128)(2,1)S(1)}, u32[]{:S(2)}) copy-start(bf16[16,64,512]{2,1,0:T(8,128)(2,1)S(1)} %gather_fusion.3) | copy-start | bytes 3145732
  180.4 29.4 %copy-start.3 = (s32[64,64]{1,0:T(8,128)S(1)}, s32[64,64]{1,0:T(8,128)}, u32[]{:S(2)}) copy-start(s32[64,64]{1,0:T(8,128)} %param.16) | copy-start | bytes 49156
  180.4 29.4 %copy-start.11 = (s32[64]{0:T(128)S(1)}, s32[64]{0:T(128)}, u32[]{:S(2)}) copy-start(s32[64]{0:T(128)} %param.17) | copy-start | bytes 772
  209.9 61.5 %copy-start.5 = (f32[64,4]{1,0:T(8,128)S(1)}, f32[64,4]{1,0:T(8,128)}, u32[]{:S(2)}) copy-start(f32[64,4]{1,0:T(8,128)} %get-tuple-element.144) | copy-start | bytes 3076
  302.8 59.5 %copy-start.4 = (f32[64,4,1,64]{3,2,1,0:T(1,128)S(1)}, f32[64,4,1,64]{3,2,1,0:T(1,128)}, u32[]{:S(2)}) copy-start(f32[64,4,1,64]{3,2,1,0:T(1,128)} %fusion.14) | copy-start | bytes 196612
  302.8 59.5 %copy-start.7 = (f32[64,4]{1,0:T(8,128)S(1)}, f32[64,4]{1,0:T(8,128)}, u32[]{:S(2)}) copy-start(f32[64,4]{1,0:T(8,128)} %convert_element_type.39) | copy-start | bytes 3076
  302.8 59.5 %copy-start.8 = (f32[64,4]{1,0:T(8,128)S(1)}, f32[64,4]{1,0:T(8,128)}, u32[]{:S(2)}) copy-start(f32[64,4]{1,0:T(8,128)} %get-tuple-element.159) | copy-start | bytes 3076
  302.8 894.0 %copy-start.6 = (bf16[256,512]{1,0:T(8,128)(2,1)S(1)}, bf16[256,512]{1,0:T(8,128)(2,1)}, u32[]{:S(2)}) copy-start(bf16[256,512]{1,0:T(8,128)(2,1)} %param.14) | copy-start | bytes 786436
  302.9 894.0 %copy-start.13 = (pred[256]{0:T(512)(128)(4,1)S(1)}, pred[256]{0:T(512)(128)(4,1)}, u32[]{:S(2)}) copy-start(pred[256]{0:T(512)(128)(4,1)} %compare_and_fusion.2) | copy-start | bytes 772
  362.3 871.0 %copy-start.1 = (bf16[512,768]{1,0:T(8,128)(2,1)S(1)}, bf16[512,768]{1,0:T(8,128)(2,1)}, u32[]{:S(2)}) copy-start(bf16[512,768]{1,0:T(8,128)(2,1)} %param.13) | copy-start | bytes 2359300
Sparse Core Ops, SparseCore 0:
  40.3 51.1 reduce-scatter.2
  1198.0 35.2 reduce-scatter.4
where the time goes:
time: 1240 us
  blocking collectives  842 us (68%)
  local copies, waits for them, and re-layouts  211 us (17%)
  waiting for transfers between devices  97 us (8%)
  other arithmetic  36.3 us (3%)
  matrix products  31.9 us (3%)
  between operations  15 us (1%)
    all_gather x1, blocking collectives, on_device(): mixed_all = lax.all_gather(mixed, 'row', axis=0, tiled=True)  833 us
    unnamed x30, local copies, waits for them, and re-layouts  51.6 us
    gather x1, local copies, waits for them, and re-layouts, score_block(): key_pool[page_ids].reshape(req_count, block_len, heads_here, HEAD_DIM)  42.6 us
    gather x1, local copies, waits for them, and re-layouts, value_block(): value_pool[page_ids].reshape(req_count, block_len, heads_here, HEAD_DIM)  42.6 us
    all_to_all x1, waiting for transfers between devices, on_device(): lax.all_to_all(outgoing, 'row', split_axis=0, concat_axis=0, tiled=True)  38 us
    reduce_scatter x1, waiting for transfers between devices, on_device(): lax.psum_scatter(jnp.dot(jnp.take(mixed_all, chosen, axis=0), w_out, pref...  35.4 us
    while x1, local copies, waits for them, and re-layouts, attend(): lax.fori_loop(0, block_count, value_block, jnp.zeros((req_count, heads_he...  26.5 us
  transfers between devices with their start and end apart: 3, of which 3 were waited for; matrix products, arithmetic and copies ran while one was open for 3% of the time, Pallas kernels for 0%

commit v1 on v0

v1 whole, which is shorter than its diff:
```python
import functools

import jax
import jax.numpy as jnp
from jax import lax
from jax.experimental import pallas as pl
from jax.experimental.pallas import tpu as pltpu
from jax.sharding import PartitionSpec as P

HEAD_DIM = 64
PAGE = 64


theta_base = 130000.0
neg_large = -1e30


def rotate(values, positions):
    half = values.shape[-1] // 2
    freqs = theta_base ** (-(jnp.arange(half, dtype=jnp.float32) * 2.0 / values.shape[-1]))
    angles = positions.astype(jnp.float32)[:, None, None] * freqs[None, None, :]
    cosine = jnp.cos(angles)
    sine = jnp.sin(angles)
    first = values[..., :half]
    second = values[..., half:]
    return jnp.concatenate(
        [first * cosine - second * sine, second * cosine + first * sine], axis=-1
    )


def paged_kernel(tbl, lens, qrow_ref, snew_ref, vrow_ref, pool_ref, land_ref,
                 out_ref, pages, scores, sems):
    i = pl.program_id(0)
    reqs = pl.num_programs(0)
    pool_n = pool_ref.shape[0]
    land_n = land_ref.shape[0]
    maxp = pages.shape[1]

    def start_request(r, slot):
        count = (lens[r] + PAGE - 1) // PAGE

        def body(j, carry):
            p = tbl[r * maxp + j]

            @pl.when(p < pool_n)
            def _():
                src = jnp.clip(p, 0, pool_n - 1)
                pltpu.make_async_copy(
                    pool_ref.at[src], pages.at[slot, j], sems.at[slot, j]
                ).start()

            @pl.when(p >= pool_n)
            def _():
                src = jnp.clip(p - pool_n, 0, land_n - 1)
                pltpu.make_async_copy(
                    land_ref.at[src], pages.at[slot, j], sems.at[slot, j]
                ).start()

            return carry

        lax.fori_loop(0, count, body, 0)

    @pl.when(i == 0)
    def _():
        start_request(0, 0)

    @pl.when(i + 1 < reqs)
    def _():
        start_request(i + 1, (i + 1) % 2)

    slot = i % 2
    length = lens[i]
    count = (length + PAGE - 1) // PAGE
    qrow = qrow_ref[0]
    rows = qrow.shape[0]
    pos = lax.broadcasted_iota(jnp.int32, (rows, PAGE), 1)

    def score_body(j, top):
        pltpu.make_async_copy(pool_ref.at[0], pages.at[slot, j], sems.at[slot, j]).wait()
        page = pages[slot, j]
        s = lax.dot_general(
            qrow, page, (((1,), (1,)), ((), ())), preferred_element_type=jnp.float32
        ) * 0.125
        s = jnp.where(j * PAGE + pos < length, s, neg_large)
        scores[j] = s
        return jnp.maximum(top, s)

    top = lax.fori_loop(0, count, score_body, jnp.full((rows, PAGE), neg_large, jnp.float32))
    snew = snew_ref[0][:, :1]
    top = jnp.maximum(jnp.max(top, axis=1, keepdims=True), snew)

    def value_body(j, carry):
        total, numer = carry
        s = scores[j]
        e = jnp.where(j * PAGE + pos < length, jnp.exp(s - top), 0.0)
        w = e.astype(jnp.bfloat16)
        numer = numer + jnp.dot(w, pages[slot, j], preferred_element_type=jnp.float32)
        return total + e, numer

    lanes = qrow.shape[1]
    total, numer = lax.fori_loop(
        0, count, value_body,
        (jnp.zeros((rows, PAGE), jnp.float32), jnp.zeros((rows, lanes), jnp.float32)),
    )
    e_new = jnp.exp(snew - top)
    total = jnp.sum(total, axis=1, keepdims=True) + e_new
    w_new = e_new.astype(jnp.bfloat16).astype(jnp.float32)
    numer = numer + w_new * vrow_ref[0]
    out_ref[0] = (numer / total).astype(out_ref.dtype)


def attend(query, key_new, value_new, table, lens, pool, landed):
    req_count, heads_here, _ = query.shape
    lanes = pool.shape[2]
    maxp = table.shape[1]
    rows = 8
    qf = query.astype(jnp.float32)
    score_new = jnp.sum(qf * key_new.astype(jnp.float32), axis=-1) * 0.125
    eye = jnp.eye(rows, heads_here, dtype=jnp.float32)
    zeros = jnp.zeros_like(qf)
    qrow = (eye[None, :, :, None, None] *
            jnp.stack([qf, zeros], axis=2)[:, None, :, :, :]).reshape(req_count, rows, lanes)
    qrow = qrow.astype(jnp.bfloat16)
    vf = value_new.astype(jnp.float32)
    vrow = (eye[None, :, :, None, None] *
            jnp.stack([zeros, vf], axis=2)[:, None, :, :, :]).reshape(req_count, rows, lanes)
    snew = jnp.zeros((req_count, rows, 128), jnp.float32) + jnp.pad(
        score_new, ((0, 0), (0, rows - heads_here)))[:, :, None]

    grid_spec = pltpu.PrefetchScalarGridSpec(
        num_scalar_prefetch=2,
        grid=(req_count,),
        in_specs=[
            pl.BlockSpec((1, rows, lanes), lambda i, t, l: (i, 0, 0)),
            pl.BlockSpec((1, rows, 128), lambda i, t, l: (i, 0, 0)),
            pl.BlockSpec((1, rows, lanes), lambda i, t, l: (i, 0, 0)),
            pl.BlockSpec(memory_space=pl.ANY),
            pl.BlockSpec(memory_space=pl.ANY),
        ],
        out_specs=pl.BlockSpec((1, rows, lanes), lambda i, t, l: (i, 0, 0)),
        scratch_shapes=[
            pltpu.VMEM((2, maxp, PAGE, lanes), jnp.bfloat16),
            pltpu.VMEM((maxp, rows, PAGE), jnp.float32),
            pltpu.SemaphoreType.DMA((2, maxp)),
        ],
    )
    out = pl.pallas_call(
        paged_kernel,
        grid_spec=grid_spec,
        out_shape=jax.ShapeDtypeStruct((req_count, rows, lanes), jnp.bfloat16),
        compiler_params=pltpu.CompilerParams(
            dimension_semantics=("arbitrary",), vmem_limit_bytes=48 * 1024 * 1024
        ),
    )(table.reshape(-1), lens, qrow, snew, vrow, pool, landed)
    out = out[:, :heads_here].reshape(req_count, heads_here, heads_here, 2, HEAD_DIM)
    picked = jnp.stack([out[:, h, h, 1] for h in range(heads_here)], axis=1)
    return picked


def on_device(xn, w_qkv, w_out, pool, page_table, lengths, mig_src, deal):
    heads_here = w_out.shape[0] // HEAD_DIM
    rows_all = xn.shape[0] * lax.axis_size("col")
    row_count = lax.axis_size("row")
    req_row = rows_all // row_count
    inverse = jnp.zeros((rows_all,), jnp.int32).at[deal].set(jnp.arange(rows_all, dtype=jnp.int32))
    gathered = lax.all_gather(xn, "col", axis=0, tiled=True)
    chosen = inverse
    projected = lax.psum_scatter(
        jnp.dot(jnp.take(gathered, chosen, axis=0), w_qkv, preferred_element_type=jnp.float32),
        "row",
        scatter_dimension=0,
        tiled=True,
    )
    projected = projected.reshape(req_row, heads_here, 3, HEAD_DIM)
    query = rotate(projected[:, :, 0], lengths).astype(jnp.bfloat16)
    key_new = rotate(projected[:, :, 1], lengths).astype(jnp.bfloat16)
    value_new = projected[:, :, 2].astype(jnp.bfloat16)
    my_row = lax.axis_index("row")
    pool_dev = pool.shape[0]
    land_dev = mig_src.shape[0] // row_count
    source_row = mig_src // pool_dev
    local_page = jnp.clip(mig_src - my_row * pool_dev, 0, pool_dev - 1)
    outgoing = jnp.where(
        (source_row == my_row)[:, None, None],
        jnp.take(pool, local_page, axis=0),
        jnp.zeros((), jnp.bfloat16),
    )
    outgoing = outgoing.reshape(row_count, land_dev, pool.shape[1], pool.shape[2])
    received = lax.all_to_all(outgoing, "row", split_axis=0, concat_axis=0, tiled=True)
    my_sources = lax.dynamic_slice_in_dim(source_row, my_row * land_dev, land_dev)
    landed = received[my_sources, jnp.arange(land_dev)]
    mixed = attend(query, key_new, value_new, page_table, lengths, pool, landed)
    mixed = mixed.reshape(req_row, heads_here * HEAD_DIM)
    mixed_all = lax.all_gather(mixed, "row", axis=0, tiled=True)
    chosen = deal
    attended = lax.psum_scatter(
        jnp.dot(
            jnp.take(mixed_all, chosen, axis=0), w_out, preferred_element_type=jnp.float32
        ).astype(jnp.bfloat16),
        "col",
        scatter_dimension=0,
        tiled=True,
    )
    return (attended, landed)


def solution(mesh):
    placed = (
        P("col", "row"),
        P("row", "col"),
        P("col", "row"),
        P("row", None, "col"),
        P("row", None),
        P("row"),
        P(),
        P(),
    )
    return jax.shard_map(
        on_device,
        mesh=mesh,
        in_specs=placed,
        out_specs=(P("col", "row"), P("row", None, "col")),
        check_vma=False,
    )
```

time: 1240 us -> 278 us (0.22)
  blocking collectives: 842 us -> 35.4 us
  local copies, waits for them, and re-layouts: 211 us -> 18.7 us
  Pallas kernels: 0 us -> 67 us
  other arithmetic: 36.3 us -> 5.84 us
  matrix products: 31.9 us -> 3.23 us
  waiting for transfers between devices: 97 us -> 124 us
    all_gather x1, blocking collectives: 833 us -> 26.1 us  [on_device(): mixed_all = lax.all_gather(mixed, 'row', axis=0, tiled=True)]
    gather x2 -> x0, local copies, waits for them, and re-layouts: 85.2 us -> none  [the longest x1 42.6 us: score_block(): key_pool[page_ids].reshape(req_count, block_len, heads_here, HEAD_DIM)]
    pallas_call x0 -> x1, Pallas kernels: none -> 67 us  [attend(): pl.pallas_call(paged_kernel, grid_spec=grid_spec, out_shape=jax.ShapeDtyp...]
    unnamed x30 -> x17, local copies, waits for them, and re-layouts: 51.6 us -> 0.15 us
    dot_general x2 -> x0, matrix products: 29.7 us -> none  [the longest x1 15 us: value_block(): jnp.einsum('rht,rthe->rhe', weights, values, preferred_element_type=jnp.f...]
    reduce_scatter x1, waiting for transfers between devices: 23.6 us -> 50.7 us  [on_device(): lax.psum_scatter(jnp.dot(jnp.take(gathered, chosen, axis=0), w_qkv, prefe...]
    while x1 -> x0, local copies, waits for them, and re-layouts: 26.5 us -> none  [attend(): lax.fori_loop(0, block_count, value_block, jnp.zeros((req_count, heads_he...]
    squeeze x1, local copies, waits for them, and re-layouts: 21.7 us -> 0.02 us  [on_device(): key_new = rotate(projected[:, :, 1], lengths).astype(jnp.bfloat16)]
where the time goes in v1:
time: 278 us; the launch traced here: 275 us
  waiting for transfers between devices  124 us (45%)
  Pallas kernels  67 us (24%)
  blocking collectives  35.4 us (13%)
  local copies, waits for them, and re-layouts  18.7 us (7%)
  between operations  14.3 us (5%)
  starting transfers between devices  6.53 us (2%)
  other arithmetic  5.84 us (2%)
  matrix products  3.23 us (1%)
    pallas_call x1, Pallas kernels, attend(): pl.pallas_call(paged_kernel, grid_spec=grid_spec, out_shape=jax.ShapeDtyp...  67 us
    reduce_scatter x1, waiting for transfers between devices, on_device(): lax.psum_scatter(jnp.dot(jnp.take(gathered, chosen, axis=0), w_qkv, prefe...  50.7 us
    all_to_all x1, waiting for transfers between devices, on_device(): lax.all_to_all(outgoing, 'row', split_axis=0, concat_axis=0, tiled=True)  38 us
    reduce_scatter x1, waiting for transfers between devices, on_device(): lax.psum_scatter(jnp.dot(jnp.take(mixed_all, chosen, axis=0), w_out, pref...  35.4 us
    all_gather x1, blocking collectives, on_device(): mixed_all = lax.all_gather(mixed, 'row', axis=0, tiled=True)  26.1 us
    all_gather x1, blocking collectives, on_device(): gathered = lax.all_gather(xn, 'col', axis=0, tiled=True)  9.32 us
    gather x1, local copies, waits for them, and re-layouts, on_device(): jnp.take(pool, local_page, axis=0)  8.56 us
    all_to_all x1, starting transfers between devices, on_device(): lax.all_to_all(outgoing, 'row', split_axis=0, concat_axis=0, tiled=True)  6.45 us
  transfers between devices with their start and end apart: 3, of which 3 were waited for; matrix products, arithmetic and copies ran while one was open for 3% of the time, Pallas kernels for 0%

profile of v1, /device:TPU:0, one launch (start us, length us, event | category | flops | bytes accessed | tf_op | source)
XLA Modules:
  0.0 275.3 jit_solution(6105809480205037778)
XLA Ops:
  7.2 0.0 copy-start
  7.2 0.7 broadcast_compare_fusion
  7.9 0.1 broadcast_in_dim.72
  8.0 0.1 broadcast_in_dim.74
  8.1 8.6 %gather_fusion.1 = bf16[64,64,512]{2,1,0:T(8,128)(2,1)} fusion(bf16[256,64,512]{2,1,0:T(8,128)(2,1)} %pool_ref.1, s32[1024]{0:T(1024)S(1)} %pad_clamp_fusion.1), kind=kCustom, calls=%fused_computation.1 | custom fusion | bytes 8388864 | tf_op jit(solution)/shard_map/jit(_take)/gather | solution.py:185
  16.7 3.9 %select_select_fusion = bf16[4,16,64,512]{3,2,1,0:T(8,128)(2,1)} fusion(bf16[4,16,64,512]{3,2,1,0:T(8,128)(2,1)} %bitcast.31, pred[4,16]{1,0:T(4,128)(4,1)S(1)} %broadcast_in_dim.74, pred[4,16]{1,0:T(4,128)(4,1)S(1)} %broadcast_in_dim.72), kind=kLoop, calls=%fused_computation.5 | loop fusion | flops 4194304 | bytes 8388736 | tf_op jit(solution)/shard_map/jit(_where)/select_n | solution.py:183
  20.6 6.4 %all-to-all-start = ((bf16[4,16,64,512]{3,2,1,0:T(8,128)(2,1)}), bf16[4,16,64,512]{3,2,1,0:T(8,128)(2,1)}, u32[]{:S(2)}, u32[]{:S(2)}) async-start(bf16[4,16,64,512]{3,2,1,0:T(8,128)(2,1)} %select_select_fusion), calls=%async_computation.1 | async-start | bytes 8388608 | tf_op jit(solution)/shard_map/all_to_all | solution.py:189
  27.0 0.0 reduce-scatter.3.cloned.1.call-start
  27.1 0.0 copy-done.5
  27.1 1.4 scatter_custom_fusion
  28.5 9.3 %all_gather.6 = bf16[256,512]{1,0:T(8,128)(2,1)S(1)} all-gather(bf16[32,512]{1,0:T(8,128)(2,1)S(1)} %copy-done.3), channel_id=1, replica_groups=mesh['row'=4,'col'=8] {'col'}, dimensions={0}, use_global_device_ids=true | all-gather | bytes 294912 | tf_op jit(solution)/shard_map/all_gather | solution.py:166
  37.8 1.2 gather_fusion
  39.0 1.3 fusion.2
  40.3 0.0 reduce-scatter.3.cloned.1.call-update
  40.3 0.0 reduce-scatter.5.cloned.1.call-start
  40.4 0.1 mul.142
  40.5 0.1 mul.143
  40.6 0.1 reshape.153.tbl
  40.7 0.1 fusion.16
  40.8 0.2 multiply_cosine_fusion
  41.0 50.7 %reduce-scatter.3.cloned.1.call-done = f32[64,768]{1,0:T(8,128)} async-done(((f32[256,768]{1,0:T(8,128)}), f32[64,768]{1,0:T(8,128)}) %reduce-scatter.3.cloned.1.call-update) | async-done | bytes 196624 | tf_op jit(solution)/shard_map/reduce_scatter | solution.py:168
  91.7 1.2 reshape.154
  92.9 0.1 slice.78
  93.1 0.2 fusion.22
  93.3 0.1 subtract_convert_fusion
  93.5 0.2 multiply_reduce_fusion
  93.7 0.1 copy.54
  93.8 0.1 fusion.6
  93.9 0.2 copy.40
  94.1 0.3 reshape.157
  94.4 0.2 pad_convert_fusion
  94.6 0.3 reshape.158
  94.9 0.2 broadcast_multiply_fusion
  95.1 38.0 %all-to-all-done = bf16[4,16,64,512]{3,2,1,0:T(8,128)(2,1)} async-done(((bf16[4,16,64,512]{3,2,1,0:T(8,128)(2,1)}), bf16[4,16,64,512]{3,2,1,0:T(8,128)(2,1)}, u32[]{:S(2)}, u32[]{:S(2)}) %all-to-all-start) | async-done | bytes 4194336 | tf_op jit(solution)/shard_map/all_to_all | solution.py:189
  133.1 2.8 %gather_fusion.2 = bf16[16,64,512]{2,1,0:T(8,128)(2,1)S(1)} fusion(bf16[4,16,64,512]{3,2,1,0:T(8,128)(2,1)} %all-to-all-done, s32[16]{0:T(128)S(1)} %fusion.16), kind=kCustom, calls=%fused_computation.2 | custom fusion | bytes 2097280 | tf_op jit(solution)/shard_map/gather | solution.py:191
  135.9 0.0 copy-start.1
  135.9 0.1 add.56.snew_ref
  136.0 67.0 %shard_map.95 = bf16[64,8,512]{2,1,0:T(8,128)(2,1)S(1)} custom-call(s32[4096]{0:T(1024)S(1)} %reshape.153.tbl, s32[64]{0:T(128)S(1)} %copy-done.2, bf16[64,8,512]{2,1,0:T(8,128)(2,1)S(1)} %get-tuple-element.19.qrow_ref, f32[64,8,128]{2,1,0:T(8,128)S(1)} %add.56.snew_ref, f32[64,8,512]{2,1,0:T(8,128)S(1)} %get-tuple-element.18.vrow_ref, ...), custom_call_target="tpu_custom_call" | custom-call | tf_op jit(solution)/shard_map/pallas_call | solution.py:147
  203.1 0.1 slice.64
  203.2 0.3 reshape.155
  203.5 0.1 fusion.21
  203.7 0.1 copy.47
  203.8 0.1 reshape.156
  203.9 26.1 %all_gather.7 = bf16[256,256]{1,0:T(8,128)(2,1)S(1)} all-gather(bf16[64,256]{1,0:T(8,128)(2,1)S(1)} %reshape.156), channel_id=1, replica_groups=mesh['row'=4,'col'=8] {'row'}, dimensions={0}, use_global_device_ids=true | all-gather | bytes 163840 | tf_op jit(solution)/shard_map/all_gather | solution.py:194
  229.9 1.2 gather_fusion.3
  231.1 1.9 convolution_convert_fusion
  233.0 0.0 reduce-scatter.5.cloned.1.call-update
  233.1 35.4 %reduce-scatter.5.cloned.1.call-done = bf16[32,512]{1,0:T(8,128)(2,1)} async-done(((bf16[256,512]{1,0:T(8,128)(2,1)}), bf16[32,512]{1,0:T(8,128)(2,1)}) %reduce-scatter.5.cloned.1.call-update) | async-done | bytes 32784 | tf_op jit(solution)/shard_map/reduce_scatter | solution.py:196
  (28 shorter events, 0.2 us)
Async XLA Ops:
  7.2 31.8 %copy-start = (bf16[512,768]{1,0:T(8,128)(2,1)S(1)}, bf16[512,768]{1,0:T(8,128)(2,1)}, u32[]{:S(2)}) copy-start(bf16[512,768]{1,0:T(8,128)(2,1)} %param.9) | copy-start | bytes 2359300
  20.6 6.5 %copy-start.5 = (s32[256]{0:T(256)S(1)}, s32[256]{0:T(256)}, u32[]{:S(2)}) copy-start(s32[256]{0:T(256)} %param.15) | copy-start | bytes 3076
  20.6 7.9 %copy-start.3 = (bf16[32,512]{1,0:T(8,128)(2,1)S(1)}, bf16[32,512]{1,0:T(8,128)(2,1)}, u32[]{:S(2)}) copy-start(bf16[32,512]{1,0:T(8,128)(2,1)} %param.8) | copy-start | bytes 98308
  20.6 112.5 %all-to-all-start = ((bf16[4,16,64,512]{3,2,1,0:T(8,128)(2,1)}), bf16[4,16,64,512]{3,2,1,0:T(8,128)(2,1)}, u32[]{:S(2)}, u32[]{:S(2)}) async-start(bf16[4,16,64,512]{3,2,1,0:T(8,128)(2,1)} %select_select_fusion), calls=%async_computation.1 | async-start | bytes 8388608 | tf_op jit(solution)/shard_map/all_to_all | solution.py:189
  27.0 13.4 %copy-start.2 = (s32[64]{0:T(128)S(1)}, s32[64]{0:T(128)}, u32[]{:S(2)}) copy-start(s32[64]{0:T(128)} %lens.1) | copy-start | bytes 772
  27.0 13.6 %copy-start.4 = (s32[64,64]{1,0:T(8,128)S(1)}, s32[64,64]{1,0:T(8,128)}, u32[]{:S(2)}) copy-start(s32[64,64]{1,0:T(8,128)} %param.12) | copy-start | bytes 49156
  27.0 64.7 %reduce-scatter.3.cloned.1.call-start = ((), (), s32[]{:S(2)}) async-start(), calls=%async_computation.3 | async-start | bytes 983040 | tf_op jit(solution)/shard_map/reduce_scatter | solution.py:168
  40.3 228.1 %reduce-scatter.5.cloned.1.call-start = ((), (), s32[]{:S(2)}) async-start(), calls=%async_computation.4 | async-start | bytes 294912 | tf_op jit(solution)/shard_map/reduce_scatter | solution.py:196
  135.9 67.2 %copy-start.1 = (bf16[16,64,512]{2,1,0:T(8,128)(2,1)}, bf16[16,64,512]{2,1,0:T(8,128)(2,1)S(1)}, u32[]{:S(2)}) copy-start(bf16[16,64,512]{2,1,0:T(8,128)(2,1)S(1)} %gather_fusion.2) | copy-start | bytes 3145732
Sparse Core Ops, SparseCore 0:
  40.5 51.2 reduce-scatter.2
  233.2 35.2 reduce-scatter.4
